TPU v7x, 256 devices: a whole 4x4x8 slice. The times are simulated.
256 devices in a mesh: ctx: 64 (over x, y_hi, z), pipe: 4 (over y_lo, core).
Axes of the slice: x: 4, y: 4 (y_hi: 2, y_lo: 2; y = y_hi * 2 + y_lo), z: 8, core: 2. Of those that a mesh axis runs over, the one named last changes fastest.
Arguments:
- inputs: bfloat16 [4, 8192, 4096], P('pipe', 'ctx'), may hold values from -16 to 16
- q_raw: bfloat16 [4, 8192, 2048], P('pipe', 'ctx'), may hold values from -6 to 6
- grad_out: bfloat16 [4, 8192, 2048], P('pipe', 'ctx'), may hold values from -6 to 6
- segments: int32 [4, 8192], P('pipe'), may hold values from 0 to 4, never falling along the last dimension, each value on 1 to 3072 neighbouring positions
- w_key: bfloat16 [4, 4096, 512], P('pipe', 'ctx'), may hold values from -0.09375 to 0.09375
- w_value: bfloat16 [4, 4096, 512], P('pipe', 'ctx'), may hold values from -0.09375 to 0.09375
- q_gain: float32 [4, 128], P('pipe'), may hold values from 0.1 to 1.9
- k_gain: float32 [4, 128], P('pipe'), may hold values from 0.1 to 1.9
Outputs:
- query_grad: bfloat16 [4, 8192, 2048], P('pipe', 'ctx')
- key_weight_grad: float32 [4, 4096, 512], P('pipe', 'ctx')
- value_weight_grad: float32 [4, 4096, 512], P('pipe', 'ctx')
- section_grad: bfloat16 [4, 8192, 4096], P('pipe', 'ctx')
Inputs may be any that keep to these rules, and one draw needn't show every extreme that they name: `segments`: along each section's sequence the document numbers never fall; every document has 1 to 3072 tokens and one has exactly 3072.
All inputs are finite; a program needn't handle non-finite values.
Results may differ from a plain program's by a relative error of at most 0.019.
Values may be sent and summed in bfloat16 or wider, within the bound.
No kernel may reach another device: no remote copies, remote signals or barrier semaphores. Data moves between devices by JAX's collectives and lax.ppermute only.
A program may use at most 128 MiB of HBM per device.

v0:
```python
import jax
import jax.numpy as jnp
from jax import lax
from jax.sharding import PartitionSpec as P

HEAD = 128
WINDOW = 768
epsilon = 1e-06
theta_base = 1000000.0


def passed_along(block, axis, distance):
    devices = range(lax.axis_size(axis))
    route = [(i - distance, i) for i in devices if i - distance in devices]
    return lax.ppermute(block, axis, route)


def shifted(shard, axis, by):
    devices = lax.axis_size(axis)
    return lax.ppermute(shard, axis, [(i, (i + by) % devices) for i in range(devices)])


def rope_tables(positions):
    half_width = HEAD // 2
    frequency = jnp.exp(
        jnp.arange(half_width, dtype=jnp.float32) * (-2.0 * jnp.log(jnp.float32(theta_base)) / HEAD)
    )
    angles = positions.astype(jnp.float32)[:, None] * frequency[None, :]
    return (jnp.cos(angles), jnp.sin(angles))


def rotate(values, cosine, sine_table):
    half_width = values.shape[-1] // 2
    front_half = values[..., :half_width]
    back_half = values[..., half_width:]
    cos_b = cosine[:, None, :]
    sin_b = sine_table[:, None, :]
    return jnp.concatenate(
        [front_half * cos_b - back_half * sin_b, back_half * cos_b + front_half * sin_b], -1
    )


def unrotate(upstream, cosine, sine_table):
    half_width = upstream.shape[-1] // 2
    front_half = upstream[..., :half_width]
    back_half = upstream[..., half_width:]
    cos_b = cosine[:, None, :]
    sin_b = sine_table[:, None, :]
    return jnp.concatenate(
        [front_half * cos_b + back_half * sin_b, back_half * cos_b - front_half * sin_b], -1
    )


def normalize(values, gain_row):
    inverse = lax.rsqrt(jnp.mean(values * values, -1, keepdims=True) + epsilon)
    return (values * inverse * gain_row, inverse)


def normalize_back(values, inverse, gain_row, upstream):
    scaled = upstream * gain_row
    cubed = inverse * inverse * inverse
    return inverse * scaled - values * cubed * jnp.mean(values * scaled, -1, keepdims=True)


def guarded(tile_work, operands):
    return tile_work(*operands)


def local(inputs, q_raw, grad_out, segments, w_key, w_value, q_gain, k_gain):
    tokens_here = inputs[0]
    tok_rows = tokens_here.shape[0]
    kv_width = w_key.shape[2]
    kv_heads = kv_width // HEAD
    q_heads = q_raw.shape[2] // HEAD
    group = q_heads // kv_heads
    score_scale = HEAD ** (-0.5)
    reach_blocks = WINDOW // tok_rows
    ctx_index = lax.axis_index("ctx")
    key_full, value_full = (
        lax.all_gather(w_key[0], "ctx", axis=0, tiled=True),
        lax.all_gather(w_value[0], "ctx", axis=0, tiled=True),
    )
    key_raw = jnp.dot(tokens_here, key_full, preferred_element_type=jnp.float32).astype(
        jnp.bfloat16
    )
    value_own = (
        jnp.dot(tokens_here, value_full, preferred_element_type=jnp.float32)
        .astype(jnp.bfloat16)
        .reshape(tok_rows, kv_heads, HEAD)
    )
    local_pos = jnp.arange(tok_rows, dtype=jnp.int32)
    positions = ctx_index * tok_rows + local_pos
    cosine, sine_table = rope_tables(positions)
    query_in = q_raw[0].astype(jnp.float32).reshape(tok_rows, q_heads, HEAD)
    query_norm, query_inv = normalize(query_in, q_gain[0])
    query_rot = rotate(query_norm, cosine, sine_table).astype(jnp.bfloat16)
    key_in = key_raw.astype(jnp.float32).reshape(tok_rows, kv_heads, HEAD)
    key_norm, key_inv = normalize(key_in, k_gain[0])
    key_rot = rotate(key_norm, cosine, sine_table).astype(jnp.bfloat16)
    own_pair = jnp.stack([key_rot, value_own])
    key_blocks = [own_pair]
    for distance in range(1, reach_blocks + 1):
        key_blocks.append(passed_along(own_pair, "ctx", distance))
    seg_all = segments[0]
    seg_query = lax.dynamic_slice_in_dim(seg_all, ctx_index * tok_rows, tok_rows)
    allowed_list = []
    for distance in range(reach_blocks + 1):
        key_pos = (ctx_index - distance) * tok_rows + local_pos
        seg_key = lax.dynamic_slice_in_dim(
            seg_all, jnp.maximum(ctx_index - distance, 0) * tok_rows, tok_rows
        )
        offset = positions[:, None] - key_pos[None, :]
        allowed = (
            (offset >= 0)
            & (offset < WINDOW)
            & (key_pos >= 0)[None, :]
            & (seg_query[:, None] == seg_key[None, :])
        )
        allowed_list.append(allowed)
    q_group = query_rot.reshape(tok_rows, kv_heads, group, HEAD)
    out_grad = grad_out[0].reshape(tok_rows, kv_heads, group, HEAD)

    def exp_block(key_pair, allowed):
        scores = (
            jnp.einsum("qgrd,kgd->grqk", q_group, key_pair[0], preferred_element_type=jnp.float32)
            * score_scale
        )
        return jnp.where(allowed, jnp.exp(scores), 0.0)

    def total_block(key_pair, allowed):
        return jnp.sum(exp_block(key_pair, allowed), -1)

    zero_total = jnp.zeros((kv_heads, group, tok_rows), jnp.float32)
    row_total = zero_total
    for distance in range(reach_blocks + 1):
        row_total = row_total + guarded(total_block, (key_blocks[distance], allowed_list[distance]))

    def prob_block(key_pair, allowed):
        prob_tile = (exp_block(key_pair, allowed) / row_total[..., None]).astype(jnp.bfloat16)
        out_tile = jnp.einsum(
            "grqk,kgd->qgrd", prob_tile, key_pair[1], preferred_element_type=jnp.float32
        )
        return (prob_tile, out_tile)

    zero_query = jnp.zeros((tok_rows, kv_heads, group, HEAD), jnp.float32)
    prob_list = []
    attn_out = zero_query
    for distance in range(reach_blocks + 1):
        prob_tile, out_tile = guarded(prob_block, (key_blocks[distance], allowed_list[distance]))
        prob_list.append(prob_tile)
        attn_out = attn_out + out_tile
    row_delta = jnp.sum(out_grad.astype(jnp.float32) * attn_out, -1).transpose(1, 2, 0)[..., None]

    def grad_block(key_pair, prob_tile):
        prob_grad = jnp.einsum(
            "qgrd,kgd->grqk", out_grad, key_pair[1], preferred_element_type=jnp.float32
        )
        score_grad = (prob_tile.astype(jnp.float32) * (prob_grad - row_delta)).astype(jnp.bfloat16)
        value_grad = jnp.einsum(
            "grqk,qgrd->kgd", prob_tile, out_grad, preferred_element_type=jnp.float32
        )
        key_grad = (
            jnp.einsum("grqk,qgrd->kgd", score_grad, q_group, preferred_element_type=jnp.float32)
            * score_scale
        )
        query_part = (
            jnp.einsum(
                "grqk,kgd->qgrd", score_grad, key_pair[0], preferred_element_type=jnp.float32
            )
            * score_scale
        )
        return (query_part, jnp.stack([key_grad, value_grad]))

    zero_pair = jnp.zeros((2, tok_rows, kv_heads, HEAD), jnp.float32)
    query_rot_grad = zero_query
    kv_total = zero_pair
    for distance in range(reach_blocks + 1):
        query_part, kv_part = guarded(grad_block, (key_blocks[distance], prob_list[distance]))
        query_rot_grad = query_rot_grad + query_part
        if distance == 0:
            kv_total = kv_part
        else:
            returned = passed_along(kv_part.astype(jnp.bfloat16), "ctx", -distance)
            kv_total = kv_total + returned.astype(jnp.float32)
    query_grad = normalize_back(
        query_in,
        query_inv,
        q_gain[0],
        unrotate(query_rot_grad.reshape(tok_rows, q_heads, HEAD), cosine, sine_table),
    )
    query_grad = query_grad.reshape(tok_rows, q_heads * HEAD).astype(jnp.bfloat16)
    key_back = normalize_back(key_in, key_inv, k_gain[0], unrotate(kv_total[0], cosine, sine_table))
    key_back = key_back.reshape(tok_rows, kv_width).astype(jnp.bfloat16)
    value_back = kv_total[1].reshape(tok_rows, kv_width).astype(jnp.bfloat16)
    both_back = jnp.concatenate([key_back, value_back], 1)
    grad_rows = lax.psum_scatter(
        lax.dot_general(
            tokens_here, both_back, (((0,), (0,)), ((), ())), preferred_element_type=jnp.float32
        ),
        "ctx",
        scatter_dimension=0,
        tiled=True,
    )
    input_grad = lax.dot_general(
        key_back, key_full, (((1,), (1,)), ((), ())), preferred_element_type=jnp.float32
    )
    input_grad = input_grad + lax.dot_general(
        value_back, value_full, (((1,), (1,)), ((), ())), preferred_element_type=jnp.float32
    )
    passed = shifted(input_grad.astype(jnp.bfloat16), "pipe", -1)
    return (
        query_grad[None],
        grad_rows[:, :kv_width][None],
        grad_rows[:, kv_width:][None],
        passed[None],
    )


def solution(mesh):
    return jax.shard_map(
        local,
        mesh=mesh,
        in_specs=(
            P("pipe", "ctx", None),
            P("pipe", "ctx", None),
            P("pipe", "ctx", None),
            P("pipe", None),
            P("pipe", "ctx", None),
            P("pipe", "ctx", None),
            P("pipe", None),
            P("pipe", None),
        ),
        out_specs=(
            P("pipe", "ctx", None),
            P("pipe", "ctx", None),
            P("pipe", "ctx", None),
            P("pipe", "ctx", None),
        ),
        check_vma=False,
    )
```

profile of v0, /device:TPU:0, one launch (start us, length us, event | category | flops | bytes accessed | tf_op | source)
XLA Modules:
  0.0 868.9 jit_solution(1845894031588987251)
XLA Ops:
  20.3 120.0 %all-gather.7.cloned.1.call-done = bf16[1,4096,512]{2,1,0:T(8,128)(2,1)} async-done(((bf16[1,64,512]{2,1,0:T(8,128)(2,1)}), bf16[1,4096,512]{2,1,0:T(8,128)(2,1)}) %all-gather.7.cloned.1.call-update) | async-done | bytes 4194320 | tf_op jit(solution)/shard_map/all_gather | solution.py:81
  140.3 2.9 fusion.76
  144.0 124.1 %all-gather.5.cloned.1.call-done = bf16[1,4096,512]{2,1,0:T(8,128)(2,1)} async-done(((bf16[1,64,512]{2,1,0:T(8,128)(2,1)}), bf16[1,4096,512]{2,1,0:T(8,128)(2,1)}) %all-gather.5.cloned.1.call-update) | async-done | bytes 4194320 | tf_op jit(solution)/shard_map/all_gather | solution.py:80
  268.1 2.9 fusion.73
  283.7 4.4 collective-permute-start.5
  288.1 6.4 collective-permute-start.4
  294.4 4.0 collective-permute-start.3
  298.4 6.3 collective-permute-start.2
  304.7 4.3 collective-permute-start.1
  313.4 2.7 collective-permute-start
  322.7 13.7 %collective-permute-done.1 = bf16[2,128,4,128]{3,1,2,0:T(8,128)(2,1)} collective-permute-done((bf16[2,128,4,128]{3,1,2,0:T(8,128)(2,1)}, bf16[2,128,4,128]{3,1,2,0:T(8,128)(2,1)}, u32[]{:S(2)}, u32[]{:S(2)}) %collective-permute-start.1) | collective-permute-done | bytes 262176 | tf_op jit(solution)/shard_map/ppermute | solution.py:15
  366.4 2.5 collective-permute-done.6
  371.0 10.9 %collective-permute-done.7 = bf16[2,128,4,128]{3,1,2,0:T(8,128)(2,1)S(1)} collective-permute-done((bf16[2,128,4,128]{3,1,2,0:T(8,128)(2,1)S(1)}, bf16[2,128,4,128]{3,1,2,0:T(8,128)(2,1)S(1)}, u32[]{:S(2)}, u32[]{:S(2)}) %collective-permute-start.7) | collective-permute-done | bytes 262176 | tf_op jit(solution)/shard_map/ppermute | solution.py:15
  382.0 9.7 %collective-permute-done.8 = bf16[2,128,4,128]{3,1,2,0:T(8,128)(2,1)S(1)} collective-permute-done((bf16[2,128,4,128]{3,1,2,0:T(8,128)(2,1)S(1)}, bf16[2,128,4,128]{3,1,2,0:T(8,128)(2,1)S(1)}, u32[]{:S(2)}, u32[]{:S(2)}) %collective-permute-start.8) | collective-permute-done | bytes 262176 | tf_op jit(solution)/shard_map/ppermute | solution.py:15
  391.7 9.5 %collective-permute-done.11 = bf16[2,128,4,128]{3,1,2,0:T(8,128)(2,1)S(1)} collective-permute-done((bf16[2,128,4,128]{3,1,2,0:T(8,128)(2,1)S(1)}, bf16[2,128,4,128]{3,1,2,0:T(8,128)(2,1)S(1)}, u32[]{:S(2)}, u32[]{:S(2)}) %collective-permute-start.11) | collective-permute-done | bytes 262176 | tf_op jit(solution)/shard_map/ppermute | solution.py:15
  405.3 9.1 %convolution_bitcast_fusion = f32[4096,1024]{0,1:T(8,128)} fusion(bf16[1,128,4096]{2,1,0:T(8,128)(2,1)S(1)} %copy-done, bf16[128,512]{1,0:T(8,128)(2,1)} %bitcast.613, bf16[128,512]{1,0:T(8,128)(2,1)S(1)} %fusion.115), kind=kOutput, calls=%fused_computation | convolution fusion | flops 1074266112 | bytes 18087936 | tf_op jit(solution)/shard_map/dot_general | solution.py:197
  414.4 17.5 %copy.546 = f32[4096,1024]{1,0:T(8,128)} copy(f32[4096,1024]{0,1:T(8,128)} %convolution_bitcast_fusion) | data formatting | bytes 33554432
  435.5 2.4 mul.515
  453.5 2.5 fusion
  459.7 2.4 concatenate.48
  462.2 3.1 fusion.105
  465.3 10.3 %collective-permute-done.12 = bf16[128,4096]{1,0:T(8,128)(2,1)} collective-permute-done((bf16[128,4096]{1,0:T(8,128)(2,1)}, bf16[128,4096]{1,0:T(8,128)(2,1)}, u32[]{:S(2)}, u32[]{:S(2)}) %collective-permute-start.12) | collective-permute-done | bytes 1048608 | tf_op jit(solution)/shard_map/ppermute | solution.py:20
  475.6 381.7 %reduce-scatter.4.cloned.1.call-done = f32[64,1024]{1,0:T(8,128)} async-done(((f32[4096,1024]{1,0:T(8,128)}), f32[64,1024]{1,0:T(8,128)}) %reduce-scatter.4.cloned.1.call-update) | async-done | bytes 262160
  860.1 2.3 copy.572
  (231 shorter events, 98.5 us)
Async XLA Ops:
  7.2 133.2 %copy-start = (bf16[1,128,4096]{2,1,0:T(8,128)(2,1)S(1)}, bf16[1,128,4096]{2,1,0:T(8,128)(2,1)}, u32[]{:S(2)}) copy-start(bf16[1,128,4096]{2,1,0:T(8,128)(2,1)} %param.8) | copy-start | bytes 3145732
  7.2 133.1 %all-gather.7.cloned.1.call-start = ((), (), s32[]{:S(2)}) async-start(), calls=%async_computation.2 | async-start | bytes 4259840 | tf_op jit(solution)/shard_map/all_gather | solution.py:81
  7.9 260.2 %all-gather.5.cloned.1.call-start = ((), (), s32[]{:S(2)}) async-start(), calls=%async_computation.1 | async-start | bytes 4259840 | tf_op jit(solution)/shard_map/all_gather | solution.py:80
  8.7 848.6 %reduce-scatter.4.cloned.1.call-start = ((), (), s32[]{:S(2)}) async-start(), calls=%async_computation.3 | async-start | bytes 17039360
  283.7 29.8 %collective-permute-start.5 = (bf16[2,128,4,128]{3,1,2,0:T(8,128)(2,1)}, bf16[2,128,4,128]{3,1,2,0:T(8,128)(2,1)}, u32[]{:S(2)}, u32[]{:S(2)}) collective-permute-start(bf16[2,128,4,128]{3,1,2,0:T(8,128)(2,1)} %pad_maximum_fusion.2), channel_id=1, source_target_pairs={{0,24},{4,28},{8,32},{12,36},{16,40},{20,44},{24,48},{28,52},{32,5... | collective-permute-start | bytes 786440 | tf_op jit(solution)/shard_map/ppermute | solution.py:15
  288.1 29.4 %collective-permute-start.4 = (bf16[2,128,4,128]{3,1,2,0:T(8,128)(2,1)}, bf16[2,128,4,128]{3,1,2,0:T(8,128)(2,1)}, u32[]{:S(2)}, u32[]{:S(2)}) collective-permute-start(bf16[2,128,4,128]{3,1,2,0:T(8,128)(2,1)} %pad_maximum_fusion.2), channel_id=1, source_target_pairs={{0,20},{4,24},{8,28},{12,32},{16,36},{20,40},{24,44},{28,48},{32,5... | collective-permute-start | bytes 786440 | tf_op jit(solution)/shard_map/ppermute | solution.py:15
  294.4 24.3 %collective-permute-start.3 = (bf16[2,128,4,128]{3,1,2,0:T(8,128)(2,1)}, bf16[2,128,4,128]{3,1,2,0:T(8,128)(2,1)}, u32[]{:S(2)}, u32[]{:S(2)}) collective-permute-start(bf16[2,128,4,128]{3,1,2,0:T(8,128)(2,1)} %pad_maximum_fusion.2), channel_id=1, source_target_pairs={{0,16},{4,20},{8,24},{12,28},{16,32},{20,36},{24,40},{28,44},{32,4... | collective-permute-start | bytes 786440 | tf_op jit(solution)/shard_map/ppermute | solution.py:15
  298.4 22.9 %collective-permute-start.2 = (bf16[2,128,4,128]{3,1,2,0:T(8,128)(2,1)}, bf16[2,128,4,128]{3,1,2,0:T(8,128)(2,1)}, u32[]{:S(2)}, u32[]{:S(2)}) collective-permute-start(bf16[2,128,4,128]{3,1,2,0:T(8,128)(2,1)} %pad_maximum_fusion.2), channel_id=1, source_target_pairs={{0,12},{4,16},{8,20},{12,24},{16,28},{20,32},{24,36},{28,40},{32,4... | collective-permute-start | bytes 786440 | tf_op jit(solution)/shard_map/ppermute | solution.py:15
  304.7 31.7 %collective-permute-start.1 = (bf16[2,128,4,128]{3,1,2,0:T(8,128)(2,1)}, bf16[2,128,4,128]{3,1,2,0:T(8,128)(2,1)}, u32[]{:S(2)}, u32[]{:S(2)}) collective-permute-start(bf16[2,128,4,128]{3,1,2,0:T(8,128)(2,1)} %pad_maximum_fusion.2), channel_id=1, source_target_pairs={{0,8},{4,12},{8,16},{12,20},{16,24},{20,28},{24,32},{28,36},{32,40... | collective-permute-start | bytes 786440 | tf_op jit(solution)/shard_map/ppermute | solution.py:15
  312.1 24.3 %copy-start.38 = (pred[128,128]{0,1:T(8,128)(4,1)S(1)}, pred[128,128]{0,1:T(8,128)(4,1)}, u32[]{:S(2)}) copy-start(pred[128,128]{0,1:T(8,128)(4,1)} %get-tuple-element.60) | copy-start | bytes 49156
  313.4 26.4 %copy-start.37 = (pred[128,128]{0,1:T(8,128)(4,1)S(1)}, pred[128,128]{0,1:T(8,128)(4,1)}, u32[]{:S(2)}) copy-start(pred[128,128]{0,1:T(8,128)(4,1)} %get-tuple-element.59) | copy-start | bytes 49156
  313.4 26.4 %collective-permute-start = (bf16[2,128,4,128]{3,1,2,0:T(8,128)(2,1)}, bf16[2,128,4,128]{3,1,2,0:T(8,128)(2,1)S(1)}, u32[]{:S(2)}, u32[]{:S(2)}) collective-permute-start(bf16[2,128,4,128]{3,1,2,0:T(8,128)(2,1)} %pad_maximum_fusion.2), channel_id=1, source_target_pairs={{0,4},{4,8},{8,12},{12,16},{16,20},{20,24},{24,28},{28,32},{32,36}... | collective-permute-start | bytes 786440 | tf_op jit(solution)/shard_map/ppermute | solution.py:15
  359.3 9.6 %collective-permute-start.6 = (bf16[2,128,4,128]{3,1,2,0:T(8,128)(2,1)S(1)}, bf16[2,128,4,128]{3,1,2,0:T(8,128)(2,1)S(1)}, u32[]{:S(2)}, u32[]{:S(2)}) collective-permute-start(bf16[2,128,4,128]{3,1,2,0:T(8,128)(2,1)S(1)} %pad_maximum_fusion.3), channel_id=1, source_target_pairs={{4,0},{8,4},{12,8},{16,12},{20,16},{24,20},{28,24},{32,28},{36,32}... | collective-permute-start | bytes 786440 | tf_op jit(solution)/shard_map/ppermute | solution.py:15
  360.6 21.3 %collective-permute-start.7 = (bf16[2,128,4,128]{3,1,2,0:T(8,128)(2,1)S(1)}, bf16[2,128,4,128]{3,1,2,0:T(8,128)(2,1)S(1)}, u32[]{:S(2)}, u32[]{:S(2)}) collective-permute-start(bf16[2,128,4,128]{3,1,2,0:T(8,128)(2,1)S(1)} %pad_maximum_fusion.4), channel_id=1, source_target_pairs={{8,0},{12,4},{16,8},{20,12},{24,16},{28,20},{32,24},{36,28},{40,32... | collective-permute-start | bytes 786440 | tf_op jit(solution)/shard_map/ppermute | solution.py:15
  362.0 29.7 %collective-permute-start.8 = (bf16[2,128,4,128]{3,1,2,0:T(8,128)(2,1)S(1)}, bf16[2,128,4,128]{3,1,2,0:T(8,128)(2,1)S(1)}, u32[]{:S(2)}, u32[]{:S(2)}) collective-permute-start(bf16[2,128,4,128]{3,1,2,0:T(8,128)(2,1)S(1)} %pad_maximum_fusion.5), channel_id=1, source_target_pairs={{12,0},{16,4},{20,8},{24,12},{28,16},{32,20},{36,24},{40,28},{44,3... | collective-permute-start | bytes 786440 | tf_op jit(solution)/shard_map/ppermute | solution.py:15
  363.3 28.4 %collective-permute-start.9 = (bf16[2,128,4,128]{3,1,2,0:T(8,128)(2,1)S(1)}, bf16[2,128,4,128]{3,1,2,0:T(8,128)(2,1)S(1)}, u32[]{:S(2)}, u32[]{:S(2)}) collective-permute-start(bf16[2,128,4,128]{3,1,2,0:T(8,128)(2,1)S(1)} %pad_maximum_fusion.6), channel_id=1, source_target_pairs={{16,0},{20,4},{24,8},{28,12},{32,16},{36,20},{40,24},{44,28},{48,3... | collective-permute-start | bytes 786440 | tf_op jit(solution)/shard_map/ppermute | solution.py:15
  364.7 27.1 %collective-permute-start.10 = (bf16[2,128,4,128]{3,1,2,0:T(8,128)(2,1)S(1)}, bf16[2,128,4,128]{3,1,2,0:T(8,128)(2,1)S(1)}, u32[]{:S(2)}, u32[]{:S(2)}) collective-permute-start(bf16[2,128,4,128]{3,1,2,0:T(8,128)(2,1)S(1)} %pad_maximum_fusion.7), channel_id=1, source_target_pairs={{20,0},{24,4},{28,8},{32,12},{36,16},{40,20},{44,24},{48,28},{52,3... | collective-permute-start | bytes 786440 | tf_op jit(solution)/shard_map/ppermute | solution.py:15
  366.0 36.4 %copy-start.22 = (f32[128,64]{1,0:T(8,128)S(1)}, f32[128,64]{1,0:T(8,128)}, u32[]{:S(2)}) copy-start(f32[128,64]{1,0:T(8,128)} %copy-done.21) | copy-start | bytes 98308
  366.0 36.4 %copy-start.25 = (f32[128,64]{1,0:T(8,128)S(1)}, f32[128,64]{1,0:T(8,128)}, u32[]{:S(2)}) copy-start(f32[128,64]{1,0:T(8,128)} %copy-done.24) | copy-start | bytes 98308
  366.4 36.1 %copy-start.43 = (f32[1,128]{1,0:T(1,128)S(1)}, f32[1,128]{1,0:T(1,128)}, u32[]{:S(2)}) copy-start(f32[1,128]{1,0:T(1,128)} %param.15) | copy-start | bytes 1540
  368.9 32.3 %collective-permute-start.11 = (bf16[2,128,4,128]{3,1,2,0:T(8,128)(2,1)S(1)}, bf16[2,128,4,128]{3,1,2,0:T(8,128)(2,1)S(1)}, u32[]{:S(2)}, u32[]{:S(2)}) collective-permute-start(bf16[2,128,4,128]{3,1,2,0:T(8,128)(2,1)S(1)} %pad_maximum_fusion.8), channel_id=1, source_target_pairs={{24,0},{28,4},{32,8},{36,12},{40,16},{44,20},{48,24},{52,28},{56,3... | collective-permute-start | bytes 786440 | tf_op jit(solution)/shard_map/ppermute | solution.py:15
  370.7 34.5 %copy-start.41 = (f32[512]{0:T(512)S(1)}, f32[512]{0:T(512)}, u32[]{:S(2)}) copy-start(f32[512]{0:T(512)} %broadcast_bitcast_fusion.1) | copy-start | bytes 6148
  455.9 19.6 %collective-permute-start.12 = (bf16[128,4096]{1,0:T(8,128)(2,1)}, bf16[128,4096]{1,0:T(8,128)(2,1)}, u32[]{:S(2)}, u32[]{:S(2)}) collective-permute-start(bf16[128,4096]{1,0:T(8,128)(2,1)} %fusion), channel_id=1, source_target_pairs={{0,3},{1,0},{2,1},{3,2},{4,7},{5,4},{6,5},{7,6},{8,11},{9,8},{10,9... | collective-permute-start | bytes 3145736 | tf_op jit(solution)/shard_map/ppermute | solution.py:20
  459.7 402.6 %copy-start.1 = (bf16[1,128,4096]{2,1,0:T(8,128)(2,1)S(1)}, bf16[1,128,4096]{2,1,0:T(8,128)(2,1)}, u32[]{:S(2)}) copy-start(bf16[1,128,4096]{2,1,0:T(8,128)(2,1)} %param.8) | copy-start | bytes 3145732
  (38 other events, 193.2 us)
Sparse Core Ops, SparseCore 0:
  11.6 128.6 all-gather.6
  143.9 124.1 all-gather.4
  432.0 425.1 reduce-scatter.3
where the time goes:
time: 871 us; the launch traced here: 869 us
  waiting for transfers between devices  687 us (79%)
  local copies, waits for them, and re-layouts  55.3 us (6%)
  matrix products  52.3 us (6%)
  starting transfers between devices  37.1 us (4%)
  other arithmetic  22 us (3%)
  between operations  14.8 us (2%)
    unnamed x4, waiting for transfers between devices  383 us
    all_gather x1, waiting for transfers between devices, local(): lax.all_gather(w_key[0], 'ctx', axis=0, tiled=True)  124 us
    all_gather x1, waiting for transfers between devices, local(): lax.all_gather(w_value[0], 'ctx', axis=0, tiled=True)  120 us
    ppermute x12, waiting for transfers between devices, passed_along(): return lax.ppermute(block, axis, route)  50 us
    ppermute x12, starting transfers between devices, passed_along(): return lax.ppermute(block, axis, route)  36 us
    unnamed x104, local copies, waits for them, and re-layouts  32.2 us
  transfers between devices with their start and end apart: 16, of which 11 were waited for; matrix products, arithmetic and copies ran while one was open for 6% of the time, Pallas kernels for 0%

commit v1 on v0

--- a/solution.py
+++ b/solution.py
@@ -7,6 +7,13 @@
 WINDOW = 768
 epsilon = 1e-06
 theta_base = 1000000.0
+
+
+def lots_all_keep_up(sheet, a_name):
+    w2 = lax.psum(1, a_name)
+    seen_now = jnp.stack([sheet] * w2, 0)
+    all_values = lax.all_to_all(seen_now, a_name, 0, 0)
+    return jnp.concatenate(all_values, 0)
 
 
 def passed_along(block, axis, distance):
@@ -77,7 +84,7 @@
     reach_blocks = WINDOW // tok_rows
     ctx_index = lax.axis_index("ctx")
     key_full, value_full = (
-        lax.all_gather(w_key[0], "ctx", axis=0, tiled=True),
+        lots_all_keep_up(w_key[0], "ctx"),
         lax.all_gather(w_value[0], "ctx", axis=0, tiled=True),
     )
     key_raw = jnp.dot(tokens_here, key_full, preferred_element_type=jnp.float32).astype(

time: 871 us -> 776 us (0.89)
  waiting for transfers between devices: 687 us -> 574 us
  starting transfers between devices: 37.1 us -> 52.1 us
    all_gather x1 -> x0, waiting for transfers between devices: 124 us -> none  [local(): lax.all_gather(w_key[0], 'ctx', axis=0, tiled=True)]
    all_to_all x0 -> x1, starting transfers between devices: none -> 13.3 us  [lots_all_keep_up(): all_values = lax.all_to_all(seen_now, a_name, 0, 0)]
    unnamed x4 -> x3, waiting for transfers between devices: 383 us -> 384 us
  transfers between devices with their start and end apart: 16 -> 16, of which waited for: 11 -> 9; matrix products, arithmetic and copies ran while one was open for 6% -> 8% of each run, Pallas kernels for 0% -> 0%
where the time goes in v1:
time: 776 us; the launch traced here: 773 us
  waiting for transfers between devices  574 us (74%)
  local copies, waits for them, and re-layouts  55.9 us (7%)
  matrix products  55.3 us (7%)
  starting transfers between devices  52.1 us (7%)
  other arithmetic  20.8 us (3%)
  between operations  15.2 us (2%)
    unnamed x3, waiting for transfers between devices  384 us
    all_gather x1, waiting for transfers between devices, local(): lax.all_gather(w_value[0], 'ctx', axis=0, tiled=True)  123 us
    ppermute x12, waiting for transfers between devices, passed_along(): return lax.ppermute(block, axis, route)  57 us
    ppermute x12, starting transfers between devices, passed_along(): return lax.ppermute(block, axis, route)  38.8 us
    unnamed x104, local copies, waits for them, and re-layouts  29.5 us
  transfers between devices with their start and end apart: 16, of which 9 were waited for; matrix products, arithmetic and copies ran while one was open for 8% of the time, Pallas kernels for 0%

profile of v1, /device:TPU:0, one launch (start us, length us, event | category | flops | bytes accessed | tf_op | source)
XLA Modules:
  0.0 773.4 jit_solution(7276952949627030441)
XLA Ops:
  7.9 3.3 stack.88
  11.2 13.3 %all-to-all-start = ((bf16[64,64,512]{2,1,0:T(8,128)(2,1)}), bf16[64,64,512]{2,1,0:T(8,128)(2,1)}, u32[]{:S(2)}, u32[]{:S(2)}) async-start(bf16[64,64,512]{2,1,0:T(8,128)(2,1)} %stack.88), calls=%async_computation | async-start | bytes 8388608 | tf_op jit(solution)/shard_map/all_to_all | solution.py:15
  34.0 123.2 %all-gather.3.cloned.1.call-done = bf16[1,4096,512]{2,1,0:T(8,128)(2,1)} async-done(((bf16[1,64,512]{2,1,0:T(8,128)(2,1)}), bf16[1,4096,512]{2,1,0:T(8,128)(2,1)}) %all-gather.3.cloned.1.call-update) | async-done | bytes 4194320 | tf_op jit(solution)/shard_map/all_gather | solution.py:88
  157.2 2.9 fusion.66
  161.0 2.9 fusion.69
  176.5 4.1 collective-permute-start.5
  180.7 5.8 collective-permute-start.4
  186.4 3.8 collective-permute-start.3
  190.3 6.7 collective-permute-start.2
  197.0 5.0 collective-permute-start
  206.4 14.2 %collective-permute-done = bf16[2,128,4,128]{3,1,2,0:T(8,128)(2,1)} collective-permute-done((bf16[2,128,4,128]{3,1,2,0:T(8,128)(2,1)}, bf16[2,128,4,128]{3,1,2,0:T(8,128)(2,1)}, u32[]{:S(2)}, u32[]{:S(2)}) %collective-permute-start) | collective-permute-done | bytes 262176 | tf_op jit(solution)/shard_map/ppermute | solution.py:22
  220.6 5.4 collective-permute-start.1
  227.3 6.0 collective-permute-done.1
  265.8 4.9 collective-permute-done.6
  272.9 9.9 %collective-permute-done.7 = bf16[2,128,4,128]{3,1,2,0:T(8,128)(2,1)S(1)} collective-permute-done((bf16[2,128,4,128]{3,1,2,0:T(8,128)(2,1)S(1)}, bf16[2,128,4,128]{3,1,2,0:T(8,128)(2,1)S(1)}, u32[]{:S(2)}, u32[]{:S(2)}) %collective-permute-start.7) | collective-permute-done | bytes 262176 | tf_op jit(solution)/shard_map/ppermute | solution.py:22
  282.8 10.0 %collective-permute-done.8 = bf16[2,128,4,128]{3,1,2,0:T(8,128)(2,1)S(1)} collective-permute-done((bf16[2,128,4,128]{3,1,2,0:T(8,128)(2,1)S(1)}, bf16[2,128,4,128]{3,1,2,0:T(8,128)(2,1)S(1)}, u32[]{:S(2)}, u32[]{:S(2)}) %collective-permute-start.8) | collective-permute-done | bytes 262176 | tf_op jit(solution)/shard_map/ppermute | solution.py:22
  292.8 11.9 %collective-permute-done.11 = bf16[2,128,4,128]{3,1,2,0:T(8,128)(2,1)S(1)} collective-permute-done((bf16[2,128,4,128]{3,1,2,0:T(8,128)(2,1)S(1)}, bf16[2,128,4,128]{3,1,2,0:T(8,128)(2,1)S(1)}, u32[]{:S(2)}, u32[]{:S(2)}) %collective-permute-start.11) | collective-permute-done | bytes 262176 | tf_op jit(solution)/shard_map/ppermute | solution.py:22
  308.7 9.1 %convolution_bitcast_fusion = f32[4096,1024]{0,1:T(8,128)} fusion(bf16[1,128,4096]{2,1,0:T(8,128)(2,1)S(1)} %copy-done, bf16[128,512]{1,0:T(8,128)(2,1)} %bitcast.608, bf16[128,512]{1,0:T(8,128)(2,1)S(1)} %fusion.106), kind=kOutput, calls=%fused_computation | convolution fusion | flops 1074266112 | bytes 18087936 | tf_op jit(solution)/shard_map/dot_general | solution.py:204
  317.9 17.5 %copy.546 = f32[4096,1024]{1,0:T(8,128)} copy(f32[4096,1024]{0,1:T(8,128)} %convolution_bitcast_fusion) | data formatting | bytes 33554432
  353.7 3.8 fusion.165
  357.5 2.5 fusion
  365.2 3.1 fusion.96
  368.3 9.9 %collective-permute-done.12 = bf16[128,4096]{1,0:T(8,128)(2,1)} collective-permute-done((bf16[128,4096]{1,0:T(8,128)(2,1)}, bf16[128,4096]{1,0:T(8,128)(2,1)}, u32[]{:S(2)}, u32[]{:S(2)}) %collective-permute-start.12) | collective-permute-done | bytes 1048608 | tf_op jit(solution)/shard_map/ppermute | solution.py:27
  378.3 383.2 %reduce-scatter.4.cloned.1.call-done = f32[64,1024]{1,0:T(8,128)} async-done(((f32[4096,1024]{1,0:T(8,128)}), f32[64,1024]{1,0:T(8,128)}) %reduce-scatter.4.cloned.1.call-update) | async-done | bytes 262160
  (231 shorter events, 95.7 us)
Async XLA Ops:
  7.2 150.1 %copy-start = (bf16[1,128,4096]{2,1,0:T(8,128)(2,1)S(1)}, bf16[1,128,4096]{2,1,0:T(8,128)(2,1)}, u32[]{:S(2)}) copy-start(bf16[1,128,4096]{2,1,0:T(8,128)(2,1)} %param.8) | copy-start | bytes 3145732
  7.2 150.0 %all-gather.3.cloned.1.call-start = ((), (), s32[]{:S(2)}) async-start(), calls=%async_computation.2 | async-start | bytes 4259840 | tf_op jit(solution)/shard_map/all_gather | solution.py:88
  11.2 149.7 %all-to-all-start = ((bf16[64,64,512]{2,1,0:T(8,128)(2,1)}), bf16[64,64,512]{2,1,0:T(8,128)(2,1)}, u32[]{:S(2)}, u32[]{:S(2)}) async-start(bf16[64,64,512]{2,1,0:T(8,128)(2,1)} %stack.88), calls=%async_computation | async-start | bytes 8388608 | tf_op jit(solution)/shard_map/all_to_all | solution.py:15
  24.5 736.9 %reduce-scatter.4.cloned.1.call-start = ((), (), s32[]{:S(2)}) async-start(), calls=%async_computation.3 | async-start | bytes 17039360
  176.5 61.8 %collective-permute-start.5 = (bf16[2,128,4,128]{3,1,2,0:T(8,128)(2,1)}, bf16[2,128,4,128]{3,1,2,0:T(8,128)(2,1)}, u32[]{:S(2)}, u32[]{:S(2)}) collective-permute-start(bf16[2,128,4,128]{3,1,2,0:T(8,128)(2,1)} %pad_maximum_fusion.2), channel_id=1, source_target_pairs={{0,24},{4,28},{8,32},{12,36},{16,40},{20,44},{24,48},{28,52},{32,5... | collective-permute-start | bytes 786440 | tf_op jit(solution)/shard_map/ppermute | solution.py:22
  180.7 56.4 %collective-permute-start.4 = (bf16[2,128,4,128]{3,1,2,0:T(8,128)(2,1)}, bf16[2,128,4,128]{3,1,2,0:T(8,128)(2,1)}, u32[]{:S(2)}, u32[]{:S(2)}) collective-permute-start(bf16[2,128,4,128]{3,1,2,0:T(8,128)(2,1)} %pad_maximum_fusion.2), channel_id=1, source_target_pairs={{0,20},{4,24},{8,28},{12,32},{16,36},{20,40},{24,44},{28,48},{32,5... | collective-permute-start | bytes 786440 | tf_op jit(solution)/shard_map/ppermute | solution.py:22
  186.4 49.3 %collective-permute-start.3 = (bf16[2,128,4,128]{3,1,2,0:T(8,128)(2,1)}, bf16[2,128,4,128]{3,1,2,0:T(8,128)(2,1)}, u32[]{:S(2)}, u32[]{:S(2)}) collective-permute-start(bf16[2,128,4,128]{3,1,2,0:T(8,128)(2,1)} %pad_maximum_fusion.2), channel_id=1, source_target_pairs={{0,16},{4,20},{8,24},{12,28},{16,32},{20,36},{24,40},{28,44},{32,4... | collective-permute-start | bytes 786440 | tf_op jit(solution)/shard_map/ppermute | solution.py:22
  190.3 44.2 %collective-permute-start.2 = (bf16[2,128,4,128]{3,1,2,0:T(8,128)(2,1)}, bf16[2,128,4,128]{3,1,2,0:T(8,128)(2,1)}, u32[]{:S(2)}, u32[]{:S(2)}) collective-permute-start(bf16[2,128,4,128]{3,1,2,0:T(8,128)(2,1)} %pad_maximum_fusion.2), channel_id=1, source_target_pairs={{0,12},{4,16},{8,20},{12,24},{16,28},{20,32},{24,36},{28,40},{32,4... | collective-permute-start | bytes 786440 | tf_op jit(solution)/shard_map/ppermute | solution.py:22
  197.0 23.6 %collective-permute-start = (bf16[2,128,4,128]{3,1,2,0:T(8,128)(2,1)}, bf16[2,128,4,128]{3,1,2,0:T(8,128)(2,1)}, u32[]{:S(2)}, u32[]{:S(2)}) collective-permute-start(bf16[2,128,4,128]{3,1,2,0:T(8,128)(2,1)} %pad_maximum_fusion.2), channel_id=1, source_target_pairs={{0,4},{4,8},{8,12},{12,16},{16,20},{20,24},{24,28},{28,32},{32,36}... | collective-permute-start | bytes 786440 | tf_op jit(solution)/shard_map/ppermute | solution.py:22
  205.0 30.7 %copy-start.39 = (pred[128,128]{0,1:T(8,128)(4,1)S(1)}, pred[128,128]{0,1:T(8,128)(4,1)}, u32[]{:S(2)}) copy-start(pred[128,128]{0,1:T(8,128)(4,1)} %get-tuple-element.62) | copy-start | bytes 49156
  205.0 32.0 %copy-start.38 = (pred[128,128]{0,1:T(8,128)(4,1)S(1)}, pred[128,128]{0,1:T(8,128)(4,1)}, u32[]{:S(2)}) copy-start(pred[128,128]{0,1:T(8,128)(4,1)} %get-tuple-element.63) | copy-start | bytes 49156
  220.6 12.7 %collective-permute-start.1 = (bf16[2,128,4,128]{3,1,2,0:T(8,128)(2,1)}, bf16[2,128,4,128]{3,1,2,0:T(8,128)(2,1)S(1)}, u32[]{:S(2)}, u32[]{:S(2)}) collective-permute-start(bf16[2,128,4,128]{3,1,2,0:T(8,128)(2,1)} %pad_maximum_fusion.2), channel_id=1, source_target_pairs={{0,8},{4,12},{8,16},{12,20},{16,24},{20,28},{24,32},{28,36},{32,40... | collective-permute-start | bytes 786440 | tf_op jit(solution)/shard_map/ppermute | solution.py:22
  258.7 12.0 %collective-permute-start.6 = (bf16[2,128,4,128]{3,1,2,0:T(8,128)(2,1)S(1)}, bf16[2,128,4,128]{3,1,2,0:T(8,128)(2,1)S(1)}, u32[]{:S(2)}, u32[]{:S(2)}) collective-permute-start(bf16[2,128,4,128]{3,1,2,0:T(8,128)(2,1)S(1)} %pad_maximum_fusion.3), channel_id=1, source_target_pairs={{4,0},{8,4},{12,8},{16,12},{20,16},{24,20},{28,24},{32,28},{36,32}... | collective-permute-start | bytes 786440 | tf_op jit(solution)/shard_map/ppermute | solution.py:22
  260.0 22.7 %collective-permute-start.7 = (bf16[2,128,4,128]{3,1,2,0:T(8,128)(2,1)S(1)}, bf16[2,128,4,128]{3,1,2,0:T(8,128)(2,1)S(1)}, u32[]{:S(2)}, u32[]{:S(2)}) collective-permute-start(bf16[2,128,4,128]{3,1,2,0:T(8,128)(2,1)S(1)} %pad_maximum_fusion.4), channel_id=1, source_target_pairs={{8,0},{12,4},{16,8},{20,12},{24,16},{28,20},{32,24},{36,28},{40,32... | collective-permute-start | bytes 786440 | tf_op jit(solution)/shard_map/ppermute | solution.py:22
  261.4 31.4 %collective-permute-start.8 = (bf16[2,128,4,128]{3,1,2,0:T(8,128)(2,1)S(1)}, bf16[2,128,4,128]{3,1,2,0:T(8,128)(2,1)S(1)}, u32[]{:S(2)}, u32[]{:S(2)}) collective-permute-start(bf16[2,128,4,128]{3,1,2,0:T(8,128)(2,1)S(1)} %pad_maximum_fusion.5), channel_id=1, source_target_pairs={{12,0},{16,4},{20,8},{24,12},{28,16},{32,20},{36,24},{40,28},{44,3... | collective-permute-start | bytes 786440 | tf_op jit(solution)/shard_map/ppermute | solution.py:22
  262.7 30.0 %collective-permute-start.9 = (bf16[2,128,4,128]{3,1,2,0:T(8,128)(2,1)S(1)}, bf16[2,128,4,128]{3,1,2,0:T(8,128)(2,1)S(1)}, u32[]{:S(2)}, u32[]{:S(2)}) collective-permute-start(bf16[2,128,4,128]{3,1,2,0:T(8,128)(2,1)S(1)} %pad_maximum_fusion.6), channel_id=1, source_target_pairs={{16,0},{20,4},{24,8},{28,12},{32,16},{36,20},{40,24},{44,28},{48,3... | collective-permute-start | bytes 786440 | tf_op jit(solution)/shard_map/ppermute | solution.py:22
  264.0 28.7 %collective-permute-start.10 = (bf16[2,128,4,128]{3,1,2,0:T(8,128)(2,1)S(1)}, bf16[2,128,4,128]{3,1,2,0:T(8,128)(2,1)S(1)}, u32[]{:S(2)}, u32[]{:S(2)}) collective-permute-start(bf16[2,128,4,128]{3,1,2,0:T(8,128)(2,1)S(1)} %pad_maximum_fusion.7), channel_id=1, source_target_pairs={{20,0},{24,4},{28,8},{32,12},{36,16},{40,20},{44,24},{48,28},{52,3... | collective-permute-start | bytes 786440 | tf_op jit(solution)/shard_map/ppermute | solution.py:22
  265.4 40.4 %copy-start.22 = (f32[128,64]{1,0:T(8,128)S(1)}, f32[128,64]{1,0:T(8,128)}, u32[]{:S(2)}) copy-start(f32[128,64]{1,0:T(8,128)} %copy-done.21) | copy-start | bytes 98308
  265.4 40.4 %copy-start.25 = (f32[128,64]{1,0:T(8,128)S(1)}, f32[128,64]{1,0:T(8,128)}, u32[]{:S(2)}) copy-start(f32[128,64]{1,0:T(8,128)} %copy-done.24) | copy-start | bytes 98308
  265.8 40.1 %copy-start.43 = (f32[1,128]{1,0:T(1,128)S(1)}, f32[1,128]{1,0:T(1,128)}, u32[]{:S(2)}) copy-start(f32[1,128]{1,0:T(1,128)} %param.15) | copy-start | bytes 1540
  270.7 33.9 %collective-permute-start.11 = (bf16[2,128,4,128]{3,1,2,0:T(8,128)(2,1)S(1)}, bf16[2,128,4,128]{3,1,2,0:T(8,128)(2,1)S(1)}, u32[]{:S(2)}, u32[]{:S(2)}) collective-permute-start(bf16[2,128,4,128]{3,1,2,0:T(8,128)(2,1)S(1)} %pad_maximum_fusion.8), channel_id=1, source_target_pairs={{24,0},{28,4},{32,8},{36,12},{40,16},{44,20},{48,24},{52,28},{56,3... | collective-permute-start | bytes 786440 | tf_op jit(solution)/shard_map/ppermute | solution.py:22
  272.5 36.0 %copy-start.41 = (f32[512]{0:T(512)S(1)}, f32[512]{0:T(512)}, u32[]{:S(2)}) copy-start(f32[512]{0:T(512)} %broadcast_bitcast_fusion.1) | copy-start | bytes 6148
  360.0 18.3 %collective-permute-start.12 = (bf16[128,4096]{1,0:T(8,128)(2,1)}, bf16[128,4096]{1,0:T(8,128)(2,1)}, u32[]{:S(2)}, u32[]{:S(2)}) collective-permute-start(bf16[128,4096]{1,0:T(8,128)(2,1)} %fusion), channel_id=1, source_target_pairs={{0,3},{1,0},{2,1},{3,2},{4,7},{5,4},{6,5},{7,6},{8,11},{9,8},{10,9... | collective-permute-start | bytes 3145736 | tf_op jit(solution)/shard_map/ppermute | solution.py:27
  362.8 403.7 %copy-start.1 = (bf16[1,128,4096]{2,1,0:T(8,128)(2,1)S(1)}, bf16[1,128,4096]{2,1,0:T(8,128)(2,1)}, u32[]{:S(2)}) copy-start(bf16[1,128,4096]{2,1,0:T(8,128)(2,1)} %param.8) | copy-start | bytes 3145732
  (38 other events, 235.7 us)
Sparse Core Ops, SparseCore 0:
  11.6 145.5 all-gather.2
  335.5 425.9 reduce-scatter.3
